TPU v7x, 32 devices: a whole 2x2x4 slice. The times are simulated.
32 devices in a mesh: groups: 2 (over x), tensor: 16 (over z, y, core).
Axes of the slice: x: 2, y: 2, z: 4, core: 2. Of those that a mesh axis runs over, the one named last changes fastest.
Arguments:
- tokens: bfloat16 [256, 8192], P(('groups', 'tensor')), parts along dimension 0, may hold values from -6 to 6
- gate_weight: bfloat16 [8192, 28672], P(None, 'tensor'), may hold values from -0.0625 to 0.0625
- up_weight: bfloat16 [8192, 28672], P(None, 'tensor'), may hold values from -0.0625 to 0.0625
- adapter_down_weight: bfloat16 [16, 8192, 64], P('tensor'), may hold values from -0.0625 to 0.0625
- adapter_up_weight: bfloat16 [16, 64, 28672], P(None, None, 'tensor'), may hold values from -0.75 to 0.75
- token_adapter_index: int32 [256, 1], P(('groups', 'tensor')), parts along dimension 0, may hold values from 0 to 15; in each aligned block of 128 rows (0 to 127, 128 to 255, ...) at most 16 rows name the same one
- adapter_slot_index: int32 [16], replicated, may hold values from 0 to 15, each once
Outputs:
- hidden: bfloat16 [256, 28672], P('groups', 'tensor'), parts along dimension 0
There are 2 independent parts, one for each index of `groups`. A program takes and returns all parts, laid end to end along the dimension named above; an argument that names none is the same for every part. Nothing has to cross between parts.
Inputs may be any that keep to these rules, and one draw needn't show every extreme that they name: `token_adapter_index`: in every draw at most 16 of all 128 tokens use one adapter, and some adapter is used by exactly 16 tokens; every adapter is used by some token. `adapter_slot_index`: A permutation; slot s is stored on the device of index s along tensor.
All inputs are finite; a program needn't handle non-finite values.
Results may differ from a plain program's by a relative error of at most 0.0039.
Values may be sent and summed in bfloat16 or wider, within the bound.
No kernel may reach another device: no remote copies, remote signals or barrier semaphores. Data moves between devices by JAX's collectives and lax.ppermute only.
A program may use at most 192 MiB of HBM per device.

v0:
```python
import jax
import jax.numpy as jnp
from jax import lax
from jax.sharding import PartitionSpec as P

CHUNKS = 2
LANES = 128


def body(
    tokens,
    gate_weight,
    up_weight,
    adapter_down_weight,
    adapter_up_weight,
    token_adapter_index,
    adapter_slot_index,
):
    me = lax.axis_index("tensor")
    rows, width = tokens.shape
    step = width // CHUNKS
    local_slot = jnp.take(adapter_slot_index, token_adapter_index[:, 0], axis=0)
    slot_cols = jnp.broadcast_to(local_slot.astype(jnp.bfloat16)[:, None], (rows, LANES))
    gate = up = low = None
    slots = None
    for c in range(CHUNKS):
        piece = tokens[:, c * step : (c + 1) * step]
        if c == CHUNKS - 1:
            piece = jnp.concatenate([piece, slot_cols], axis=1)
        gathered = lax.all_gather(piece, "tensor", axis=0, tiled=True)
        if c == CHUNKS - 1:
            slots = gathered[:, step].astype(jnp.int32)
            gathered = gathered[:, :step]
        g = jnp.dot(
            gathered, gate_weight[c * step : (c + 1) * step], preferred_element_type=jnp.float32
        )
        u = jnp.dot(
            gathered, up_weight[c * step : (c + 1) * step], preferred_element_type=jnp.float32
        )
        d = jnp.dot(
            gathered,
            adapter_down_weight[0, c * step : (c + 1) * step],
            preferred_element_type=jnp.float32,
        )
        gate = g if gate is None else gate + g
        up = u if up is None else up + u
        low = d if low is None else low + d
    mine = slots == me
    low = jnp.where(mine[:, None], low, 0.0).astype(jnp.bfloat16)
    spread = lax.all_gather(low, "tensor", axis=0, tiled=False)
    delta = jnp.einsum("str,srh->th", spread, adapter_up_weight, preferred_element_type=jnp.float32)
    return (jax.nn.silu(gate) * (up + delta)).astype(jnp.bfloat16)


def solution(mesh):
    in_specs = (
        P(("groups", "tensor"), None),
        P(None, "tensor"),
        P(None, "tensor"),
        P("tensor", None, None),
        P(None, None, "tensor"),
        P(("groups", "tensor"), None),
        P(),
    )
    out_specs = P("groups", "tensor")
    return jax.shard_map(body, mesh=mesh, in_specs=in_specs, out_specs=out_specs, check_vma=False)
```

profile of v0, /device:TPU:0, one launch (start us, length us, event | category | flops | bytes accessed | tf_op | source)
XLA Modules:
  0.0 148.9 jit_solution(2792847004383480132)
XLA Ops:
  6.5 0.0 copy-start
  6.5 0.0 all-gather.4.cloned.1.call-start
  6.5 1.5 %fusion.40 = (bf16[8,4096]{1,0:T(8,128)(2,1)}, bf16[8,4096]{1,0:T(8,128)(2,1)S(1)}) fusion(bf16[8,8192]{1,0:T(8,128)(2,1)} %param.7), kind=kLoop, calls=%fused_computation.36 | loop fusion | bytes 262144 | tf_op jit(solution)/shard_map/slice | solution.py:27
  8.0 0.0 all-gather.4.cloned.1.call-update
  8.1 0.0 all-gather.6.cloned.1.call-start
  8.1 0.7 fusion.39
  8.8 0.0 copy-done
  8.8 0.6 gather_fusion
  9.4 0.7 convert_bitcast_fusion
  10.1 0.1 broadcast_in_dim.26
  10.2 0.6 pad_maximum_fusion
  10.8 0.0 all-gather.6.cloned.1.call-update
  10.8 39.3 %all-gather.4.cloned.1.call-done = bf16[128,4096]{1,0:T(8,128)(2,1)} async-done(((bf16[8,4096]{1,0:T(8,128)(2,1)}), bf16[128,4096]{1,0:T(8,128)(2,1)}) %all-gather.4.cloned.1.call-update) | async-done | bytes 1048592 | tf_op jit(solution)/shard_map/all_gather | solution.py:30
  50.2 1.8 %fusion.34 = f32[128,64]{0,1:T(8,128)S(1)} fusion(bf16[128,4096]{1,0:T(8,128)(2,1)} %all-gather.4.cloned.1.call-done, bf16[1,8192,64]{1,2,0:T(8,128)(2,1)} %param.10), kind=kOutput, calls=%fused_computation.24 | convolution fusion | flops 67108864 | bytes 1605632 | tf_op jit(solution)/shard_map/dot_general | solution.py:40
  52.0 37.4 %all-gather.6.cloned.1.call-done = bf16[128,4224]{1,0:T(8,128)(2,1)} async-done(((bf16[8,4224]{1,0:T(8,128)(2,1)}), bf16[128,4224]{1,0:T(8,128)(2,1)}) %all-gather.6.cloned.1.call-update) | async-done | bytes 1081360 | tf_op jit(solution)/shard_map/all_gather | solution.py:30
  89.4 0.0 copy-start.3
  89.4 1.0 fusion.38
  90.4 1.8 %fusion.29 = bf16[128,64]{0,1:T(8,128)(2,1)S(1)} fusion(f32[128,64]{0,1:T(8,128)S(1)} %fusion.34, bf16[128,4224]{1,0:T(8,128)(2,1)} %all-gather.6.cloned.1.call-done, bf16[1,8192,64]{1,2,0:T(8,128)(2,1)} %param.10, pred[128]{0:T(512)(128)(4,1)S(1)} %fusion.38), kind=kOutput, calls=%fused_computation.19 | convolution fusion | flops 67133440 | bytes 1622144 | tf_op jit(solution)/shard_map/dot_general | solution.py:40
  92.2 20.1 %all-gather = bf16[2048,64]{0,1:T(8,128)(2,1)S(1)} all-gather(bf16[128,64]{0,1:T(8,128)(2,1)S(1)} %fusion.29), channel_id=2, replica_groups=mesh['groups'=2,'tensor'=16] {'tensor'}, dimensions={0}, use_global_device_ids=true | all-gather | bytes 278528 | tf_op jit(solution)/shard_map/all_gather | solution.py:50
  112.4 6.8 %fusion = f32[128,1792]{1,0:T(8,128)S(1)} fusion(bf16[8192,1792]{1,0:T(8,128)(2,1)} %param.9, bf16[128,4224]{1,0:T(8,128)(2,1)} %all-gather.6.cloned.1.call-done), kind=kOutput, calls=%fused_computation.1 | convolution fusion | flops 1879048192 | bytes 16646144 | tf_op jit(solution)/shard_map/dot_general | solution.py:37
  119.2 0.0 copy-done.3
  119.2 0.0 copy-start.2
  119.2 6.5 %fusion.4 = f32[128,1792]{1,0:T(8,128)S(1)} fusion(bf16[8192,1792]{1,0:T(8,128)(2,1)} %param.8, bf16[128,4224]{1,0:T(8,128)(2,1)S(1)} %copy-done.3), kind=kOutput, calls=%fused_computation.5 | convolution fusion | flops 1879048192 | bytes 16646144 | tf_op jit(solution)/shard_map/dot_general | solution.py:34
  125.7 0.0 copy-done.2
  125.7 6.5 %fusion.13 = f32[128,1792]{1,0:T(8,128)S(1)} fusion(f32[128,1792]{1,0:T(8,128)S(1)} %fusion.4, bf16[128,4096]{1,0:T(8,128)(2,1)S(1)} %copy-done.2, bf16[8192,1792]{1,0:T(8,128)(2,1)} %param.8), kind=kOutput, calls=%fused_computation.12 | convolution fusion | flops 1879277568 | bytes 17563648 | tf_op jit(solution)/shard_map/dot_general | solution.py:34
  132.2 0.0 copy-start.4
  132.2 0.0 copy-start.1
  132.2 6.6 %fusion.16 = f32[128,1792]{1,0:T(8,128)S(1)} fusion(f32[128,1792]{1,0:T(8,128)S(1)} %fusion, bf16[128,4096]{1,0:T(8,128)(2,1)S(1)} %copy-done.2, bf16[8192,1792]{1,0:T(8,128)(2,1)} %param.9), kind=kOutput, calls=%fused_computation.13 | convolution fusion | flops 1879277568 | bytes 17563648 | tf_op jit(solution)/shard_map/dot_general | solution.py:37
  138.9 0.0 copy-done.4
  138.9 3.2 %fusion.25 = bf16[128,1792]{1,0:T(8,128)(2,1)} fusion(f32[128,1792]{1,0:T(8,128)S(1)} %fusion.16, bf16[16,128,64]{1,0,2:T(8,128)(2,1)S(1)} %bitcast.31, bf16[16,64,1792]{2,1,0:T(8,128)(2,1)S(1)} %copy-done.4, f32[128,1792]{1,0:T(8,128)S(1)} %fusion.13), kind=kOutput, calls=%fused_computation.16 | convolution fusion | flops 471367680 | bytes 6225920 | tf_op jit(solution)/shard_map/str,srh->th/dot_general | solution.py:51
  142.1 0.0 copy-done.1
  (2 shorter events, 0.0 us)
Async XLA Ops:
  6.5 2.3 %copy-start = (s32[16]{0:T(128)S(1)}, s32[16]{0:T(128)}, u32[]{:S(2)}) copy-start(s32[16]{0:T(128)} %param.13) | copy-start | bytes 196
  6.5 43.7 %all-gather.4.cloned.1.call-start = ((), (), s32[]{:S(2)}) async-start(), calls=%async_computation | async-start | bytes 1114112 | tf_op jit(solution)/shard_map/all_gather | solution.py:30
  8.1 81.3 %all-gather.6.cloned.1.call-start = ((), (), s32[]{:S(2)}) async-start(), calls=%async_computation.1 | async-start | bytes 1148928 | tf_op jit(solution)/shard_map/all_gather | solution.py:30
  89.4 29.8 %copy-start.3 = (bf16[128,4224]{1,0:T(8,128)(2,1)S(1)}, bf16[128,4224]{1,0:T(8,128)(2,1)}, u32[]{:S(2)}) copy-start(bf16[128,4224]{1,0:T(8,128)(2,1)} %all-gather.6.cloned.1.call-done) | copy-start | bytes 3244036
  119.2 6.6 %copy-start.2 = (bf16[128,4096]{1,0:T(8,128)(2,1)S(1)}, bf16[128,4096]{1,0:T(8,128)(2,1)}, u32[]{:S(2)}) copy-start(bf16[128,4096]{1,0:T(8,128)(2,1)} %all-gather.4.cloned.1.call-done) | copy-start | bytes 3145732
  132.2 6.7 %copy-start.4 = (bf16[16,64,1792]{2,1,0:T(8,128)(2,1)S(1)}, bf16[16,64,1792]{2,1,0:T(8,128)(2,1)}, u32[]{:S(2)}) copy-start(bf16[16,64,1792]{2,1,0:T(8,128)(2,1)} %param.11) | copy-start | bytes 11010052
  132.2 9.8 %copy-start.1 = (s32[16]{0:T(128)S(1)}, s32[16]{0:T(128)}, u32[]{:S(2)}) copy-start(s32[16]{0:T(128)} %param.13) | copy-start | bytes 196
Sparse Core Ops, SparseCore 0:
  9.5 40.6 all-gather.3
  52.4 36.9 all-gather.5
where the time goes:
time: 149 us
  waiting for transfers between devices  76.7 us (51%)
  matrix products  33.3 us (22%)
  blocking collectives  20.1 us (13%)
  between operations  13.5 us (9%)
  other arithmetic  2.93 us (2%)
  local copies, waits for them, and re-layouts  2.29 us (2%)
    all_gather x2, waiting for transfers between devices, body(): gathered = lax.all_gather(piece, 'tensor', axis=0, tiled=True)  76.7 us
    all_gather x1, blocking collectives, body(): spread = lax.all_gather(low, 'tensor', axis=0, tiled=False)  20.1 us
    dot_general x2, matrix products, body(): jnp.dot(gathered, up_weight[c * step:(c + 1) * step], preferred_element_t...  13.4 us
    dot_general x2, matrix products, body(): jnp.dot(gathered, gate_weight[c * step:(c + 1) * step], preferred_element...  13 us
    dot_general x2, matrix products, body(): jnp.dot(gathered, adapter_down_weight[0, c * step:(c + 1) * step], prefer...  3.68 us
    dot_general x1, matrix products, body(): jnp.einsum('str,srh->th', spread, adapter_up_weight, preferred_element_ty...  3.19 us
  transfers between devices with their start and end apart: 2, of which 2 were waited for; matrix products, arithmetic and copies ran while one was open for 3% of the time, Pallas kernels for 0%

commit v1 on v0

--- a/solution.py
+++ b/solution.py
@@ -5,6 +5,12 @@
 
 CHUNKS = 2
 LANES = 128
+
+
+def in_order(blocks, dim):
+    shape = list(blocks.shape[1:])
+    shape[dim] *= blocks.shape[0]
+    return jnp.moveaxis(blocks, 0, dim).reshape(shape)
 
 
 def body(
@@ -27,7 +33,19 @@
         piece = tokens[:, c * step : (c + 1) * step]
         if c == CHUNKS - 1:
             piece = jnp.concatenate([piece, slot_cols], axis=1)
-        gathered = lax.all_gather(piece, "tensor", axis=0, tiled=True)
+        size = lax.axis_size("tensor")
+        pairs = [(i, (i + 1) % size) for i in range(size)]
+        back = [(b, a) for a, b in pairs]
+        lower, upper = ([], [])
+        for k in range(size - 1):
+            if k % 2 == 0:
+                lower.append(lax.ppermute(lower[-1] if lower else piece, "tensor", pairs))
+            else:
+                upper.append(lax.ppermute(upper[-1] if upper else piece, "tensor", back))
+        blocks = jnp.stack([*lower[::-1], piece, *upper])
+        shift = lax.axis_index("tensor") - len(lower)
+        blocks = blocks[(jnp.arange(size) - shift) % size]
+        gathered = in_order(blocks, 0)
         if c == CHUNKS - 1:
             slots = gathered[:, step].astype(jnp.int32)
             gathered = gathered[:, :step]

time: 149 us -> 122 us (0.82)
  waiting for transfers between devices: 76.7 us -> 12.2 us
  starting transfers between devices: 0.04 us -> 54.2 us
  between operations: 13.5 us -> 0.35 us
  blocking collectives: 20.1 us -> 18 us
  other arithmetic: 2.93 us -> 1.39 us
    all_gather x2 -> x0, waiting for transfers between devices: 76.7 us -> none  [body(): gathered = lax.all_gather(piece, 'tensor', axis=0, tiled=True)]
    ppermute x0 -> x30, starting transfers between devices: none -> 54.2 us  [the longest x14 50.4 us: body(): upper.append(lax.ppermute(upper[-1] if upper else piece, 'tensor', back))]
    ppermute x0 -> x30, waiting for transfers between devices: none -> 12.2 us  [the longest x16 7.77 us: body(): lower.append(lax.ppermute(lower[-1] if lower else piece, 'tensor', pairs))]
    all_gather x1, blocking collectives: 20.1 us -> 18 us  [body(): spread = lax.all_gather(low, 'tensor', axis=0, tiled=False)]
    dot_general x2, matrix products: 3.68 us -> 2.09 us  [body(): jnp.dot(gathered, adapter_down_weight[0, c * step:(c + 1) * step], prefer...]
  transfers between devices with their start and end apart: 2 -> 30, of which waited for: 2 -> 8; matrix products, arithmetic and copies ran while one was open for 3% -> 2% of each run, Pallas kernels for 0% -> 0%
where the time goes in v1:
time: 122 us
  starting transfers between devices  54.2 us (44%)
  matrix products  32.3 us (26%)
  blocking collectives  18 us (15%)
  waiting for transfers between devices  12.2 us (10%)
  local copies, waits for them, and re-layouts  3.37 us (3%)
  other arithmetic  1.39 us (1%)
    ppermute x14, starting transfers between devices, body(): upper.append(lax.ppermute(upper[-1] if upper else piece, 'tensor', back))  50.4 us
    all_gather x1, blocking collectives, body(): spread = lax.all_gather(low, 'tensor', axis=0, tiled=False)  18 us
    dot_general x2, matrix products, body(): jnp.dot(gathered, up_weight[c * step:(c + 1) * step], preferred_element_t...  14.7 us
    dot_general x2, matrix products, body(): jnp.dot(gathered, gate_weight[c * step:(c + 1) * step], preferred_element...  13.1 us
    ppermute x16, waiting for transfers between devices, body(): lower.append(lax.ppermute(lower[-1] if lower else piece, 'tensor', pairs))  7.77 us
    ppermute x14, waiting for transfers between devices, body(): upper.append(lax.ppermute(upper[-1] if upper else piece, 'tensor', back))  4.47 us
    ppermute x16, starting transfers between devices, body(): lower.append(lax.ppermute(lower[-1] if lower else piece, 'tensor', pairs))  3.7 us
  transfers between devices with their start and end apart: 30, of which 8 were waited for; matrix products, arithmetic and copies ran while one was open for 2% of the time, Pallas kernels for 0%

profile of v1, /device:TPU:0, one launch (start us, length us, event | category | flops | bytes accessed | tf_op | source)
XLA Modules:
  0.0 121.8 jit_solution(17737146347545487994)
XLA Ops:
  0.0 0.9 fusion.44
  0.9 0.5 collective-permute-start
  1.4 0.7 fusion.43
  2.1 0.6 gather_fusion.1
  2.7 0.7 convert_bitcast_fusion
  3.4 0.1 broadcast_in_dim.28
  3.5 2.6 %collective-permute-start.15 = (bf16[8,4224]{1,0:T(8,128)(2,1)S(1)}, bf16[8,4224]{1,0:T(8,128)(2,1)S(1)}, u32[]{:S(2)}, u32[]{:S(2)}) collective-permute-start(bf16[8,4224]{1,0:T(8,128)(2,1)S(1)} %pad_maximum_fusion), channel_id=1, source_target_pairs={{0,1},{1,2},{2,3},{3,4},{4,5},{5,6},{6,7},{7,8},{8,9},{9,10},{10,1... | collective-permute-start | bytes 202760 | tf_op jit(solution)/shard_map/ppermute | solution.py:42
  6.1 2.2 %collective-permute-done = bf16[8,4096]{1,0:T(8,128)(2,1)S(1)} collective-permute-done((bf16[8,4096]{1,0:T(8,128)(2,1)S(1)}, bf16[8,4096]{1,0:T(8,128)(2,1)S(1)}, u32[]{:S(2)}, u32[]{:S(2)}) %collective-permute-start) | collective-permute-done | bytes 65568 | tf_op jit(solution)/shard_map/ppermute | solution.py:42
  8.4 0.0 collective-permute-start.1
  8.4 4.4 %collective-permute-start.23 = (bf16[8,4224]{1,0:T(8,128)(2,1)S(1)}, bf16[8,4224]{1,0:T(8,128)(2,1)S(1)}, u32[]{:S(2)}, u32[]{:S(2)}) collective-permute-start(bf16[8,4224]{1,0:T(8,128)(2,1)S(1)} %pad_maximum_fusion), channel_id=1, source_target_pairs={{1,0},{2,1},{3,2},{4,3},{5,4},{6,5},{7,6},{8,7},{9,8},{10,9},{11,1... | collective-permute-start | bytes 202760 | tf_op jit(solution)/shard_map/ppermute | solution.py:44
  12.8 0.0 collective-permute-start.16
  12.8 4.4 %collective-permute-start.8 = (bf16[8,4096]{1,0:T(8,128)(2,1)S(1)}, bf16[8,4096]{1,0:T(8,128)(2,1)S(1)}, u32[]{:S(2)}, u32[]{:S(2)}) collective-permute-start(bf16[8,4096]{1,0:T(8,128)(2,1)S(1)} %get-tuple-element.5), channel_id=1, source_target_pairs={{1,0},{2,1},{3,2},{4,3},{5,4},{6,5},{7,6},{8,7},{9,8},{10,9},{11,1... | collective-permute-start | bytes 196616 | tf_op jit(solution)/shard_map/ppermute | solution.py:44
  17.3 4.4 %collective-permute-start.24 = (bf16[8,4224]{1,0:T(8,128)(2,1)S(1)}, bf16[8,4224]{1,0:T(8,128)(2,1)S(1)}, u32[]{:S(2)}, u32[]{:S(2)}) collective-permute-start(bf16[8,4224]{1,0:T(8,128)(2,1)S(1)} %collective-permute-done.23), channel_id=1, source_target_pairs={{1,0},{2,1},{3,2},{4,3},{5,4},{6,5},{7,6},{8,7},{9,8},{10,9},{11,1... | collective-permute-start | bytes 202760 | tf_op jit(solution)/shard_map/ppermute | solution.py:44
  21.7 4.4 %collective-permute-start.9 = (bf16[8,4096]{1,0:T(8,128)(2,1)S(1)}, bf16[8,4096]{1,0:T(8,128)(2,1)S(1)}, u32[]{:S(2)}, u32[]{:S(2)}) collective-permute-start(bf16[8,4096]{1,0:T(8,128)(2,1)S(1)} %collective-permute-done.8), channel_id=1, source_target_pairs={{1,0},{2,1},{3,2},{4,3},{5,4},{6,5},{7,6},{8,7},{9,8},{10,9},{11,1... | collective-permute-start | bytes 196616 | tf_op jit(solution)/shard_map/ppermute | solution.py:44
  26.2 4.4 %collective-permute-start.25 = (bf16[8,4224]{1,0:T(8,128)(2,1)S(1)}, bf16[8,4224]{1,0:T(8,128)(2,1)S(1)}, u32[]{:S(2)}, u32[]{:S(2)}) collective-permute-start(bf16[8,4224]{1,0:T(8,128)(2,1)S(1)} %collective-permute-done.24), channel_id=1, source_target_pairs={{1,0},{2,1},{3,2},{4,3},{5,4},{6,5},{7,6},{8,7},{9,8},{10,9},{11,1... | collective-permute-start | bytes 202760 | tf_op jit(solution)/shard_map/ppermute | solution.py:44
  30.6 4.4 %collective-permute-start.10 = (bf16[8,4096]{1,0:T(8,128)(2,1)S(1)}, bf16[8,4096]{1,0:T(8,128)(2,1)S(1)}, u32[]{:S(2)}, u32[]{:S(2)}) collective-permute-start(bf16[8,4096]{1,0:T(8,128)(2,1)S(1)} %collective-permute-done.9), channel_id=1, source_target_pairs={{1,0},{2,1},{3,2},{4,3},{5,4},{6,5},{7,6},{8,7},{9,8},{10,9},{11,1... | collective-permute-start | bytes 196616 | tf_op jit(solution)/shard_map/ppermute | solution.py:44
  35.1 4.4 %collective-permute-start.26 = (bf16[8,4224]{1,0:T(8,128)(2,1)S(1)}, bf16[8,4224]{1,0:T(8,128)(2,1)S(1)}, u32[]{:S(2)}, u32[]{:S(2)}) collective-permute-start(bf16[8,4224]{1,0:T(8,128)(2,1)S(1)} %collective-permute-done.25), channel_id=1, source_target_pairs={{1,0},{2,1},{3,2},{4,3},{5,4},{6,5},{7,6},{8,7},{9,8},{10,9},{11,1... | collective-permute-start | bytes 202760 | tf_op jit(solution)/shard_map/ppermute | solution.py:44
  39.5 4.4 %collective-permute-start.11 = (bf16[8,4096]{1,0:T(8,128)(2,1)S(1)}, bf16[8,4096]{1,0:T(8,128)(2,1)S(1)}, u32[]{:S(2)}, u32[]{:S(2)}) collective-permute-start(bf16[8,4096]{1,0:T(8,128)(2,1)S(1)} %collective-permute-done.10), channel_id=1, source_target_pairs={{1,0},{2,1},{3,2},{4,3},{5,4},{6,5},{7,6},{8,7},{9,8},{10,9},{11,1... | collective-permute-start | bytes 196616 | tf_op jit(solution)/shard_map/ppermute | solution.py:44
  44.0 1.9 %collective-permute-done.11 = bf16[8,4096]{1,0:T(8,128)(2,1)S(1)} collective-permute-done((bf16[8,4096]{1,0:T(8,128)(2,1)S(1)}, bf16[8,4096]{1,0:T(8,128)(2,1)S(1)}, u32[]{:S(2)}, u32[]{:S(2)}) %collective-permute-start.11) | collective-permute-done | bytes 65568 | tf_op jit(solution)/shard_map/ppermute | solution.py:44
  45.9 4.5 %collective-permute-start.12 = (bf16[8,4096]{1,0:T(8,128)(2,1)S(1)}, bf16[8,4096]{1,0:T(8,128)(2,1)S(1)}, u32[]{:S(2)}, u32[]{:S(2)}) collective-permute-start(bf16[8,4096]{1,0:T(8,128)(2,1)S(1)} %collective-permute-done.11), channel_id=1, source_target_pairs={{1,0},{2,1},{3,2},{4,3},{5,4},{6,5},{7,6},{8,7},{9,8},{10,9},{11,1... | collective-permute-start | bytes 196616 | tf_op jit(solution)/shard_map/ppermute | solution.py:44
  50.4 0.0 collective-permute-start.27
  50.4 0.5 collective-permute-start.20
  50.9 0.1 collective-permute-start.6
  51.0 1.3 %collective-permute-done.12 = bf16[8,4096]{1,0:T(8,128)(2,1)S(1)} collective-permute-done((bf16[8,4096]{1,0:T(8,128)(2,1)S(1)}, bf16[8,4096]{1,0:T(8,128)(2,1)S(1)}, u32[]{:S(2)}, u32[]{:S(2)}) %collective-permute-start.12) | collective-permute-done | bytes 65568 | tf_op jit(solution)/shard_map/ppermute | solution.py:44
  52.3 4.5 %collective-permute-start.13 = (bf16[8,4096]{1,0:T(8,128)(2,1)S(1)}, bf16[8,4096]{1,0:T(8,128)(2,1)S(1)}, u32[]{:S(2)}, u32[]{:S(2)}) collective-permute-start(bf16[8,4096]{1,0:T(8,128)(2,1)S(1)} %collective-permute-done.12), channel_id=1, source_target_pairs={{1,0},{2,1},{3,2},{4,3},{5,4},{6,5},{7,6},{8,7},{9,8},{10,9},{11,1... | collective-permute-start | bytes 196616 | tf_op jit(solution)/shard_map/ppermute | solution.py:44
  56.8 0.7 collective-permute-start.28
  57.5 0.2 collective-permute-done.6
  57.7 1.0 collective-permute-done.13
  58.7 4.5 %collective-permute-start.14 = (bf16[8,4096]{1,0:T(8,128)(2,1)S(1)}, bf16[8,4096]{1,0:T(8,128)(2,1)S(1)}, u32[]{:S(2)}, u32[]{:S(2)}) collective-permute-start(bf16[8,4096]{1,0:T(8,128)(2,1)S(1)} %collective-permute-done.13), channel_id=1, source_target_pairs={{1,0},{2,1},{3,2},{4,3},{5,4},{6,5},{7,6},{8,7},{9,8},{10,9},{11,1... | collective-permute-start | bytes 196616 | tf_op jit(solution)/shard_map/ppermute | solution.py:44
  63.1 0.7 collective-permute-start.29
  63.9 0.0 collective-permute-done.21
  63.9 0.7 collective-permute-done.7
  64.8 0.2 collective-permute-done.14
  65.1 0.6 gather_fusion
  65.7 4.6 %collective-permute-done.22 = bf16[8,4224]{1,0:T(8,128)(2,1)S(1)} collective-permute-done((bf16[8,4224]{1,0:T(8,128)(2,1)S(1)}, bf16[8,4224]{1,0:T(8,128)(2,1)S(1)}, u32[]{:S(2)}, u32[]{:S(2)}) %collective-permute-start.22) | collective-permute-done | bytes 67616 | tf_op jit(solution)/shard_map/ppermute | solution.py:42
  70.6 0.7 gather_fusion.2
  71.3 0.0 copy-start.4
  71.3 0.1 copy.16
  71.4 1.6 %fusion.33 = f32[128,64]{0,1:T(8,128)S(1)} fusion(bf16[128,4224]{1,0:T(8,128)(2,1)S(1)} %bitcast.97, bf16[1,8192,64]{1,2,0:T(8,128)(2,1)} %param.10), kind=kOutput, calls=%fused_computation.25 | convolution fusion | flops 67108864 | bytes 1605632 | tf_op jit(solution)/shard_map/dot_general | solution.py:58
  73.0 0.5 fusion.29
  73.5 18.0 %all-gather = bf16[2048,64]{0,1:T(8,128)(2,1)S(1)} all-gather(bf16[128,64]{0,1:T(8,128)(2,1)S(1)} %fusion.29), channel_id=2, replica_groups=mesh['groups'=2,'tensor'=16] {'tensor'}, dimensions={0}, use_global_device_ids=true | all-gather | bytes 278528 | tf_op jit(solution)/shard_map/all_gather | solution.py:68
  91.6 6.5 %fusion = f32[128,1792]{1,0:T(8,128)S(1)} fusion(bf16[8192,1792]{1,0:T(8,128)(2,1)} %param.9, bf16[128,4224]{1,0:T(8,128)(2,1)S(1)} %bitcast.98), kind=kOutput, calls=%fused_computation.3 | convolution fusion | flops 1879048192 | bytes 16646144 | tf_op jit(solution)/shard_map/dot_general | solution.py:55
  98.0 6.5 %fusion.4 = f32[128,1792]{1,0:T(8,128)S(1)} fusion(bf16[8192,1792]{1,0:T(8,128)(2,1)} %param.8, bf16[128,4224]{1,0:T(8,128)(2,1)S(1)} %bitcast.99), kind=kOutput, calls=%fused_computation.7 | convolution fusion | flops 1879048192 | bytes 16646144 | tf_op jit(solution)/shard_map/dot_general | solution.py:52
  104.5 0.0 copy-start.2
  104.5 6.7 %fusion.13 = f32[128,1792]{1,0:T(8,128)S(1)} fusion(f32[128,1792]{1,0:T(8,128)S(1)} %fusion.4, bf16[8192,1792]{1,0:T(8,128)(2,1)} %param.8, bf16[16,8,4096]{2,1,0:T(8,128)(2,1)S(1)} %gather_fusion), kind=kOutput, calls=%fused_computation.14 | convolution fusion | flops 1879277568 | bytes 17563648 | tf_op jit(solution)/shard_map/dot_general | solution.py:52
  111.2 2.3 %fusion.10 = f32[128,1792]{1,0:T(8,128)S(1)} fusion(bf16[16,128,64]{1,0,2:T(8,128)(2,1)S(1)} %bitcast.100, bf16[16,64,1792]{2,1,0:T(8,128)(2,1)S(1)} %copy-done.2), kind=kOutput, calls=%fused_computation.13 | convolution fusion | flops 469762048 | bytes 4849664 | tf_op jit(solution)/shard_map/str,srh->th/dot_general | solution.py:69
  113.6 0.0 copy-start.1
  113.6 8.2 %fusion.25 = bf16[128,1792]{1,0:T(8,128)(2,1)} fusion(f32[128,1792]{1,0:T(8,128)S(1)} %fusion.10, f32[128,1792]{1,0:T(8,128)S(1)} %fusion, bf16[8192,1792]{1,0:T(8,128)(2,1)} %param.9, bf16[16,8,4096]{2,1,0:T(8,128)(2,1)S(1)} %gather_fusion, f32[128,1792]{1,0:T(8,128)S(1)} %fusion.13), kind=kOutput, calls=%fused_computation.18 | convolution fusion | flops 1880883200 | bytes 18939904 | tf_op jit(solution)/shard_map/dot_general | solution.py:55
  (76 shorter events, 0.5 us)
Async XLA Ops:
  0.0 2.1 %copy-start = (s32[16]{0:T(128)S(1)}, s32[16]{0:T(128)}, u32[]{:S(2)}) copy-start(s32[16]{0:T(128)} %param.13) | copy-start | bytes 196
  0.0 64.7 %copy-start.3 = (bf16[8,8192]{1,0:T(8,128)(2,1)S(1)}, bf16[8,8192]{1,0:T(8,128)(2,1)}, u32[]{:S(2)}) copy-start(bf16[8,8192]{1,0:T(8,128)(2,1)} %param.7) | copy-start | bytes 393220
  0.9 7.4 %collective-permute-start = (bf16[8,4096]{1,0:T(8,128)(2,1)S(1)}, bf16[8,4096]{1,0:T(8,128)(2,1)S(1)}, u32[]{:S(2)}, u32[]{:S(2)}) collective-permute-start(bf16[8,4096]{1,0:T(8,128)(2,1)S(1)} %get-tuple-element.5), channel_id=1, source_target_pairs={{0,1},{1,2},{2,3},{3,4},{4,5},{5,6},{6,7},{7,8},{8,9},{9,10},{10,1... | collective-permute-start | bytes 196616 | tf_op jit(solution)/shard_map/ppermute | solution.py:42
  3.5 9.3 %collective-permute-start.15 = (bf16[8,4224]{1,0:T(8,128)(2,1)S(1)}, bf16[8,4224]{1,0:T(8,128)(2,1)S(1)}, u32[]{:S(2)}, u32[]{:S(2)}) collective-permute-start(bf16[8,4224]{1,0:T(8,128)(2,1)S(1)} %pad_maximum_fusion), channel_id=1, source_target_pairs={{0,1},{1,2},{2,3},{3,4},{4,5},{5,6},{6,7},{7,8},{8,9},{9,10},{10,1... | collective-permute-start | bytes 202760 | tf_op jit(solution)/shard_map/ppermute | solution.py:42
  8.4 8.9 %collective-permute-start.1 = (bf16[8,4096]{1,0:T(8,128)(2,1)S(1)}, bf16[8,4096]{1,0:T(8,128)(2,1)S(1)}, u32[]{:S(2)}, u32[]{:S(2)}) collective-permute-start(bf16[8,4096]{1,0:T(8,128)(2,1)S(1)} %collective-permute-done), channel_id=1, source_target_pairs={{0,1},{1,2},{2,3},{3,4},{4,5},{5,6},{6,7},{7,8},{8,9},{9,10},{10,1... | collective-permute-start | bytes 196616 | tf_op jit(solution)/shard_map/ppermute | solution.py:42
  8.4 8.9 %collective-permute-start.23 = (bf16[8,4224]{1,0:T(8,128)(2,1)S(1)}, bf16[8,4224]{1,0:T(8,128)(2,1)S(1)}, u32[]{:S(2)}, u32[]{:S(2)}) collective-permute-start(bf16[8,4224]{1,0:T(8,128)(2,1)S(1)} %pad_maximum_fusion), channel_id=1, source_target_pairs={{1,0},{2,1},{3,2},{4,3},{5,4},{6,5},{7,6},{8,7},{9,8},{10,9},{11,1... | collective-permute-start | bytes 202760 | tf_op jit(solution)/shard_map/ppermute | solution.py:44
  12.8 8.9 %collective-permute-start.16 = (bf16[8,4224]{1,0:T(8,128)(2,1)S(1)}, bf16[8,4224]{1,0:T(8,128)(2,1)S(1)}, u32[]{:S(2)}, u32[]{:S(2)}) collective-permute-start(bf16[8,4224]{1,0:T(8,128)(2,1)S(1)} %collective-permute-done.15), channel_id=1, source_target_pairs={{0,1},{1,2},{2,3},{3,4},{4,5},{5,6},{6,7},{7,8},{8,9},{9,10},{10,1... | collective-permute-start | bytes 202760 | tf_op jit(solution)/shard_map/ppermute | solution.py:42
  12.8 8.9 %collective-permute-start.8 = (bf16[8,4096]{1,0:T(8,128)(2,1)S(1)}, bf16[8,4096]{1,0:T(8,128)(2,1)S(1)}, u32[]{:S(2)}, u32[]{:S(2)}) collective-permute-start(bf16[8,4096]{1,0:T(8,128)(2,1)S(1)} %get-tuple-element.5), channel_id=1, source_target_pairs={{1,0},{2,1},{3,2},{4,3},{5,4},{6,5},{7,6},{8,7},{9,8},{10,9},{11,1... | collective-permute-start | bytes 196616 | tf_op jit(solution)/shard_map/ppermute | solution.py:44
  17.3 8.9 %collective-permute-start.2 = (bf16[8,4096]{1,0:T(8,128)(2,1)S(1)}, bf16[8,4096]{1,0:T(8,128)(2,1)S(1)}, u32[]{:S(2)}, u32[]{:S(2)}) collective-permute-start(bf16[8,4096]{1,0:T(8,128)(2,1)S(1)} %collective-permute-done.1), channel_id=1, source_target_pairs={{0,1},{1,2},{2,3},{3,4},{4,5},{5,6},{6,7},{7,8},{8,9},{9,10},{10,1... | collective-permute-start | bytes 196616 | tf_op jit(solution)/shard_map/ppermute | solution.py:42
  17.3 8.9 %collective-permute-start.24 = (bf16[8,4224]{1,0:T(8,128)(2,1)S(1)}, bf16[8,4224]{1,0:T(8,128)(2,1)S(1)}, u32[]{:S(2)}, u32[]{:S(2)}) collective-permute-start(bf16[8,4224]{1,0:T(8,128)(2,1)S(1)} %collective-permute-done.23), channel_id=1, source_target_pairs={{1,0},{2,1},{3,2},{4,3},{5,4},{6,5},{7,6},{8,7},{9,8},{10,9},{11,1... | collective-permute-start | bytes 202760 | tf_op jit(solution)/shard_map/ppermute | solution.py:44
  21.7 8.9 %collective-permute-start.17 = (bf16[8,4224]{1,0:T(8,128)(2,1)S(1)}, bf16[8,4224]{1,0:T(8,128)(2,1)S(1)}, u32[]{:S(2)}, u32[]{:S(2)}) collective-permute-start(bf16[8,4224]{1,0:T(8,128)(2,1)S(1)} %collective-permute-done.16), channel_id=1, source_target_pairs={{0,1},{1,2},{2,3},{3,4},{4,5},{5,6},{6,7},{7,8},{8,9},{9,10},{10,1... | collective-permute-start | bytes 202760 | tf_op jit(solution)/shard_map/ppermute | solution.py:42
  21.7 8.9 %collective-permute-start.9 = (bf16[8,4096]{1,0:T(8,128)(2,1)S(1)}, bf16[8,4096]{1,0:T(8,128)(2,1)S(1)}, u32[]{:S(2)}, u32[]{:S(2)}) collective-permute-start(bf16[8,4096]{1,0:T(8,128)(2,1)S(1)} %collective-permute-done.8), channel_id=1, source_target_pairs={{1,0},{2,1},{3,2},{4,3},{5,4},{6,5},{7,6},{8,7},{9,8},{10,9},{11,1... | collective-permute-start | bytes 196616 | tf_op jit(solution)/shard_map/ppermute | solution.py:44
  26.2 8.9 %collective-permute-start.3 = (bf16[8,4096]{1,0:T(8,128)(2,1)S(1)}, bf16[8,4096]{1,0:T(8,128)(2,1)S(1)}, u32[]{:S(2)}, u32[]{:S(2)}) collective-permute-start(bf16[8,4096]{1,0:T(8,128)(2,1)S(1)} %collective-permute-done.2), channel_id=1, source_target_pairs={{0,1},{1,2},{2,3},{3,4},{4,5},{5,6},{6,7},{7,8},{8,9},{9,10},{10,1... | collective-permute-start | bytes 196616 | tf_op jit(solution)/shard_map/ppermute | solution.py:42
  26.2 8.9 %collective-permute-start.25 = (bf16[8,4224]{1,0:T(8,128)(2,1)S(1)}, bf16[8,4224]{1,0:T(8,128)(2,1)S(1)}, u32[]{:S(2)}, u32[]{:S(2)}) collective-permute-start(bf16[8,4224]{1,0:T(8,128)(2,1)S(1)} %collective-permute-done.24), channel_id=1, source_target_pairs={{1,0},{2,1},{3,2},{4,3},{5,4},{6,5},{7,6},{8,7},{9,8},{10,9},{11,1... | collective-permute-start | bytes 202760 | tf_op jit(solution)/shard_map/ppermute | solution.py:44
  30.6 8.9 %collective-permute-start.18 = (bf16[8,4224]{1,0:T(8,128)(2,1)S(1)}, bf16[8,4224]{1,0:T(8,128)(2,1)S(1)}, u32[]{:S(2)}, u32[]{:S(2)}) collective-permute-start(bf16[8,4224]{1,0:T(8,128)(2,1)S(1)} %collective-permute-done.17), channel_id=1, source_target_pairs={{0,1},{1,2},{2,3},{3,4},{4,5},{5,6},{6,7},{7,8},{8,9},{9,10},{10,1... | collective-permute-start | bytes 202760 | tf_op jit(solution)/shard_map/ppermute | solution.py:42
  30.6 8.9 %collective-permute-start.10 = (bf16[8,4096]{1,0:T(8,128)(2,1)S(1)}, bf16[8,4096]{1,0:T(8,128)(2,1)S(1)}, u32[]{:S(2)}, u32[]{:S(2)}) collective-permute-start(bf16[8,4096]{1,0:T(8,128)(2,1)S(1)} %collective-permute-done.9), channel_id=1, source_target_pairs={{1,0},{2,1},{3,2},{4,3},{5,4},{6,5},{7,6},{8,7},{9,8},{10,9},{11,1... | collective-permute-start | bytes 196616 | tf_op jit(solution)/shard_map/ppermute | solution.py:44
  35.1 8.9 %collective-permute-start.4 = (bf16[8,4096]{1,0:T(8,128)(2,1)S(1)}, bf16[8,4096]{1,0:T(8,128)(2,1)S(1)}, u32[]{:S(2)}, u32[]{:S(2)}) collective-permute-start(bf16[8,4096]{1,0:T(8,128)(2,1)S(1)} %collective-permute-done.3), channel_id=1, source_target_pairs={{0,1},{1,2},{2,3},{3,4},{4,5},{5,6},{6,7},{7,8},{8,9},{9,10},{10,1... | collective-permute-start | bytes 196616 | tf_op jit(solution)/shard_map/ppermute | solution.py:42
  35.1 15.3 %collective-permute-start.26 = (bf16[8,4224]{1,0:T(8,128)(2,1)S(1)}, bf16[8,4224]{1,0:T(8,128)(2,1)S(1)}, u32[]{:S(2)}, u32[]{:S(2)}) collective-permute-start(bf16[8,4224]{1,0:T(8,128)(2,1)S(1)} %collective-permute-done.25), channel_id=1, source_target_pairs={{1,0},{2,1},{3,2},{4,3},{5,4},{6,5},{7,6},{8,7},{9,8},{10,9},{11,1... | collective-permute-start | bytes 202760 | tf_op jit(solution)/shard_map/ppermute | solution.py:44
  39.5 10.9 %collective-permute-start.19 = (bf16[8,4224]{1,0:T(8,128)(2,1)S(1)}, bf16[8,4224]{1,0:T(8,128)(2,1)S(1)}, u32[]{:S(2)}, u32[]{:S(2)}) collective-permute-start(bf16[8,4224]{1,0:T(8,128)(2,1)S(1)} %collective-permute-done.18), channel_id=1, source_target_pairs={{0,1},{1,2},{2,3},{3,4},{4,5},{5,6},{6,7},{7,8},{8,9},{9,10},{10,1... | collective-permute-start | bytes 202760 | tf_op jit(solution)/shard_map/ppermute | solution.py:42
  39.5 6.3 %collective-permute-start.11 = (bf16[8,4096]{1,0:T(8,128)(2,1)S(1)}, bf16[8,4096]{1,0:T(8,128)(2,1)S(1)}, u32[]{:S(2)}, u32[]{:S(2)}) collective-permute-start(bf16[8,4096]{1,0:T(8,128)(2,1)S(1)} %collective-permute-done.10), channel_id=1, source_target_pairs={{1,0},{2,1},{3,2},{4,3},{5,4},{6,5},{7,6},{8,7},{9,8},{10,9},{11,1... | collective-permute-start | bytes 196616 | tf_op jit(solution)/shard_map/ppermute | solution.py:44
  44.0 6.9 %collective-permute-start.5 = (bf16[8,4096]{1,0:T(8,128)(2,1)S(1)}, bf16[8,4096]{1,0:T(8,128)(2,1)S(1)}, u32[]{:S(2)}, u32[]{:S(2)}) collective-permute-start(bf16[8,4096]{1,0:T(8,128)(2,1)S(1)} %collective-permute-done.4), channel_id=1, source_target_pairs={{0,1},{1,2},{2,3},{3,4},{4,5},{5,6},{6,7},{7,8},{8,9},{9,10},{10,1... | collective-permute-start | bytes 196616 | tf_op jit(solution)/shard_map/ppermute | solution.py:42
  45.9 6.4 %collective-permute-start.12 = (bf16[8,4096]{1,0:T(8,128)(2,1)S(1)}, bf16[8,4096]{1,0:T(8,128)(2,1)S(1)}, u32[]{:S(2)}, u32[]{:S(2)}) collective-permute-start(bf16[8,4096]{1,0:T(8,128)(2,1)S(1)} %collective-permute-done.11), channel_id=1, source_target_pairs={{1,0},{2,1},{3,2},{4,3},{5,4},{6,5},{7,6},{8,7},{9,8},{10,9},{11,1... | collective-permute-start | bytes 196616 | tf_op jit(solution)/shard_map/ppermute | solution.py:44
  50.4 6.4 %collective-permute-start.27 = (bf16[8,4224]{1,0:T(8,128)(2,1)S(1)}, bf16[8,4224]{1,0:T(8,128)(2,1)S(1)}, u32[]{:S(2)}, u32[]{:S(2)}) collective-permute-start(bf16[8,4224]{1,0:T(8,128)(2,1)S(1)} %collective-permute-done.26), channel_id=1, source_target_pairs={{1,0},{2,1},{3,2},{4,3},{5,4},{6,5},{7,6},{8,7},{9,8},{10,9},{11,1... | collective-permute-start | bytes 202760 | tf_op jit(solution)/shard_map/ppermute | solution.py:44
  50.4 7.1 %collective-permute-start.20 = (bf16[8,4224]{1,0:T(8,128)(2,1)S(1)}, bf16[8,4224]{1,0:T(8,128)(2,1)S(1)}, u32[]{:S(2)}, u32[]{:S(2)}) collective-permute-start(bf16[8,4224]{1,0:T(8,128)(2,1)S(1)} %collective-permute-done.19), channel_id=1, source_target_pairs={{0,1},{1,2},{2,3},{3,4},{4,5},{5,6},{6,7},{7,8},{8,9},{9,10},{10,1... | collective-permute-start | bytes 202760 | tf_op jit(solution)/shard_map/ppermute | solution.py:42
  50.9 6.8 %collective-permute-start.6 = (bf16[8,4096]{1,0:T(8,128)(2,1)S(1)}, bf16[8,4096]{1,0:T(8,128)(2,1)S(1)}, u32[]{:S(2)}, u32[]{:S(2)}) collective-permute-start(bf16[8,4096]{1,0:T(8,128)(2,1)S(1)} %collective-permute-done.5), channel_id=1, source_target_pairs={{0,1},{1,2},{2,3},{3,4},{4,5},{5,6},{6,7},{7,8},{8,9},{9,10},{10,1... | collective-permute-start | bytes 196616 | tf_op jit(solution)/shard_map/ppermute | solution.py:42
  52.3 6.4 %collective-permute-start.13 = (bf16[8,4096]{1,0:T(8,128)(2,1)S(1)}, bf16[8,4096]{1,0:T(8,128)(2,1)S(1)}, u32[]{:S(2)}, u32[]{:S(2)}) collective-permute-start(bf16[8,4096]{1,0:T(8,128)(2,1)S(1)} %collective-permute-done.12), channel_id=1, source_target_pairs={{1,0},{2,1},{3,2},{4,3},{5,4},{6,5},{7,6},{8,7},{9,8},{10,9},{11,1... | collective-permute-start | bytes 196616 | tf_op jit(solution)/shard_map/ppermute | solution.py:44
  56.8 6.4 %collective-permute-start.28 = (bf16[8,4224]{1,0:T(8,128)(2,1)S(1)}, bf16[8,4224]{1,0:T(8,128)(2,1)S(1)}, u32[]{:S(2)}, u32[]{:S(2)}) collective-permute-start(bf16[8,4224]{1,0:T(8,128)(2,1)S(1)} %collective-permute-done.27), channel_id=1, source_target_pairs={{1,0},{2,1},{3,2},{4,3},{5,4},{6,5},{7,6},{8,7},{9,8},{10,9},{11,1... | collective-permute-start | bytes 202760 | tf_op jit(solution)/shard_map/ppermute | solution.py:44
  57.5 6.4 %collective-permute-start.21 = (bf16[8,4224]{1,0:T(8,128)(2,1)S(1)}, bf16[8,4224]{1,0:T(8,128)(2,1)S(1)}, u32[]{:S(2)}, u32[]{:S(2)}) collective-permute-start(bf16[8,4224]{1,0:T(8,128)(2,1)S(1)} %collective-permute-done.20), channel_id=1, source_target_pairs={{0,1},{1,2},{2,3},{3,4},{4,5},{5,6},{6,7},{7,8},{8,9},{9,10},{10,1... | collective-permute-start | bytes 202760 | tf_op jit(solution)/shard_map/ppermute | solution.py:42
  57.6 6.9 %collective-permute-start.7 = (bf16[8,4096]{1,0:T(8,128)(2,1)S(1)}, bf16[8,4096]{1,0:T(8,128)(2,1)S(1)}, u32[]{:S(2)}, u32[]{:S(2)}) collective-permute-start(bf16[8,4096]{1,0:T(8,128)(2,1)S(1)} %collective-permute-done.6), channel_id=1, source_target_pairs={{0,1},{1,2},{2,3},{3,4},{4,5},{5,6},{6,7},{7,8},{8,9},{9,10},{10,1... | collective-permute-start | bytes 196616 | tf_op jit(solution)/shard_map/ppermute | solution.py:42
  58.7 6.4 %collective-permute-start.14 = (bf16[8,4096]{1,0:T(8,128)(2,1)S(1)}, bf16[8,4096]{1,0:T(8,128)(2,1)S(1)}, u32[]{:S(2)}, u32[]{:S(2)}) collective-permute-start(bf16[8,4096]{1,0:T(8,128)(2,1)S(1)} %collective-permute-done.13), channel_id=1, source_target_pairs={{1,0},{2,1},{3,2},{4,3},{5,4},{6,5},{7,6},{8,7},{9,8},{10,9},{11,1... | collective-permute-start | bytes 196616 | tf_op jit(solution)/shard_map/ppermute | solution.py:44
  63.1 7.4 %collective-permute-start.29 = (bf16[8,4224]{1,0:T(8,128)(2,1)S(1)}, bf16[8,4224]{1,0:T(8,128)(2,1)S(1)}, u32[]{:S(2)}, u32[]{:S(2)}) collective-permute-start(bf16[8,4224]{1,0:T(8,128)(2,1)S(1)} %collective-permute-done.28), channel_id=1, source_target_pairs={{1,0},{2,1},{3,2},{4,3},{5,4},{6,5},{7,6},{8,7},{9,8},{10,9},{11,1... | collective-permute-start | bytes 202760 | tf_op jit(solution)/shard_map/ppermute | solution.py:44
  63.9 6.4 %collective-permute-start.22 = (bf16[8,4224]{1,0:T(8,128)(2,1)S(1)}, bf16[8,4224]{1,0:T(8,128)(2,1)S(1)}, u32[]{:S(2)}, u32[]{:S(2)}) collective-permute-start(bf16[8,4224]{1,0:T(8,128)(2,1)S(1)} %collective-permute-done.21), channel_id=1, source_target_pairs={{0,1},{1,2},{2,3},{3,4},{4,5},{5,6},{6,7},{7,8},{8,9},{9,10},{10,1... | collective-permute-start | bytes 202760 | tf_op jit(solution)/shard_map/ppermute | solution.py:42
  71.3 1.7 %copy-start.4 = (bf16[1,8192,64]{1,2,0:T(8,128)(2,1)S(1)}, bf16[1,8192,64]{1,2,0:T(8,128)(2,1)}, u32[]{:S(2)}) copy-start(bf16[1,8192,64]{1,2,0:T(8,128)(2,1)} %param.10) | copy-start | bytes 3145732
  104.5 6.7 %copy-start.2 = (bf16[16,64,1792]{2,1,0:T(8,128)(2,1)S(1)}, bf16[16,64,1792]{2,1,0:T(8,128)(2,1)}, u32[]{:S(2)}) copy-start(bf16[16,64,1792]{2,1,0:T(8,128)(2,1)} %param.11) | copy-start | bytes 11010052
  113.6 8.3 %copy-start.1 = (s32[16]{0:T(128)S(1)}, s32[16]{0:T(128)}, u32[]{:S(2)}) copy-start(s32[16]{0:T(128)} %param.13) | copy-start | bytes 196
